TPU v7x, 512 devices: a whole 4x8x8 slice. The times are simulated.
512 devices in a mesh: group: 8 (over z_lo, core), dp: 8 (over y), tensor: 8 (over z_hi, x).
Axes of the slice: x: 4, y: 8, z: 8 (z_hi: 2, z_lo: 4; z = z_hi * 4 + z_lo), core: 2. Of those that a mesh axis runs over, the one named last changes fastest.
Arguments:
- keyvalue_local: float32 [8, 2, 4096, 1024], P('group', None, 'dp', 'tensor'), may hold values from -6 to 6
- keyvalue_anchor: float32 [2, 4096, 1024], P(None, 'dp', 'tensor'), may hold values from -6 to 6
- keyvalue_state: float32 [2, 4096, 1024], P(None, 'dp', 'tensor'), may hold values from -6 to 6
- router_local: float32 [8, 4096, 8], P('group', 'dp'), may hold values from -6 to 6
- router_anchor: float32 [4096, 8], P('dp'), may hold values from -6 to 6
- router_state: float32 [4096, 8], P('dp'), may hold values from -6 to 6
- gain_local: float32 [8, 2, 4096], P('group', None, 'dp'), may hold values from -6 to 6
- gain_anchor: float32 [2, 4096], P(None, 'dp'), may hold values from -6 to 6
- gain_state: float32 [2, 4096], P(None, 'dp'), may hold values from -6 to 6
- embed_local: float32 [8, 1000, 4096], P('group', 'dp', 'tensor'), may hold values from -6 to 6
- embed_anchor: float32 [1000, 4096], P('dp', 'tensor'), may hold values from -6 to 6
- embed_state: float32 [1000, 4096], P('dp', 'tensor'), may hold values from -6 to 6
- embed_basis: float32 [4096, 64], P('tensor'), may hold values from -0.25 to 0.25
- outer_rate: float32 [], replicated, may hold values from 0.5 to 1
Outputs:
- keyvalue_average: float32 [2, 4096, 1024], P(None, 'dp', 'tensor')
- keyvalue_momentum: float32 [2, 4096, 1024], P(None, 'dp', 'tensor')
- keyvalue_updated: float32 [2, 4096, 1024], P(None, 'dp', 'tensor')
- router_average: float32 [4096, 8], P('dp')
- router_momentum: float32 [4096, 8], P('dp')
- router_updated: float32 [4096, 8], P('dp')
- gain_average: float32 [2, 4096], P(None, 'dp')
- gain_momentum: float32 [2, 4096], P(None, 'dp')
- gain_updated: float32 [2, 4096], P(None, 'dp')
- embed_average: float32 [1000, 4096], P('dp', 'tensor')
- embed_momentum: float32 [1000, 4096], P('dp', 'tensor')
- embed_updated: float32 [1000, 4096], P('dp', 'tensor')
All inputs are finite; a program needn't handle non-finite values.
Results may differ from a plain program's by a relative error of at most 0.0001.
Values sent between devices are 32-bit elements; how exact they have to be, the bound alone decides.
No kernel may reach another device: no remote copies, remote signals or barrier semaphores. Data moves between devices by JAX's collectives and lax.ppermute only.
A program may use at most 64 MiB of HBM per device.

v0:
```python
import jax
import jax.numpy as jnp
from jax import lax
from jax.sharding import PartitionSpec as P


def nesterov(average, state, anchor, outer_rate):
    momentum = 0.5 * state + average
    updated = anchor - outer_rate * (average + 0.5 * momentum)
    return (average, momentum, updated)


def owned_slice(whole, position, count, axis_dim):
    return lax.dynamic_slice_in_dim(whole, position * count, count, axis_dim)


def local(
    keyvalue_local,
    keyvalue_anchor,
    keyvalue_state,
    router_local,
    router_anchor,
    router_state,
    gain_local,
    gain_anchor,
    gain_state,
    embed_local,
    embed_anchor,
    embed_state,
    embed_basis,
    outer_rate,
):
    groups = lax.axis_size("group")
    keyvalue_diff = keyvalue_anchor - keyvalue_local[0]
    router_diff = router_anchor - router_local[0]
    gain_diff = gain_anchor - gain_local[0]
    keyvalue_sum, router_sum, gain_sum = (
        lax.psum_scatter(keyvalue_diff, "group", scatter_dimension=1, tiled=True),
        lax.psum_scatter(router_diff, "group", scatter_dimension=0, tiled=True),
        lax.psum_scatter(gain_diff, "group", scatter_dimension=1, tiled=True),
    )
    position = lax.axis_index("group")
    keyvalue_rows = keyvalue_anchor.shape[1] // groups
    router_rows = router_anchor.shape[0] // groups
    gain_rows = gain_anchor.shape[1] // groups
    keyvalue_part = nesterov(
        keyvalue_sum / groups,
        owned_slice(keyvalue_state, position, keyvalue_rows, 1),
        owned_slice(keyvalue_anchor, position, keyvalue_rows, 1),
        outer_rate,
    )
    router_part = nesterov(
        router_sum / groups,
        owned_slice(router_state, position, router_rows, 0),
        owned_slice(router_anchor, position, router_rows, 0),
        outer_rate,
    )
    gain_part = nesterov(
        gain_sum / groups,
        owned_slice(gain_state, position, gain_rows, 1),
        owned_slice(gain_anchor, position, gain_rows, 1),
        outer_rate,
    )
    gathered = (
        lax.all_gather(keyvalue_part[0], "group", axis=1, tiled=True),
        lax.all_gather(keyvalue_part[1], "group", axis=1, tiled=True),
        lax.all_gather(keyvalue_part[2], "group", axis=1, tiled=True),
        lax.all_gather(router_part[0], "group", axis=0, tiled=True),
        lax.all_gather(router_part[1], "group", axis=0, tiled=True),
        lax.all_gather(router_part[2], "group", axis=0, tiled=True),
        lax.all_gather(gain_part[0], "group", axis=1, tiled=True),
        lax.all_gather(gain_part[1], "group", axis=1, tiled=True),
        lax.all_gather(gain_part[2], "group", axis=1, tiled=True),
    )
    keyvalue_out = gathered[0:3]
    router_out = gathered[3:6]
    gain_out = gathered[6:9]
    partial_factors = jnp.dot(
        embed_anchor - embed_local[0],
        embed_basis,
        precision=lax.Precision.HIGHEST,
        preferred_element_type=jnp.float32,
    )
    factors = lax.psum(partial_factors, ("group", "tensor"))
    factors = factors / groups
    embed_average = jnp.dot(
        factors, embed_basis.T, precision=lax.Precision.HIGHEST, preferred_element_type=jnp.float32
    )
    embed_out = nesterov(embed_average, embed_state, embed_anchor, outer_rate)
    return (
        keyvalue_out[0],
        keyvalue_out[1],
        keyvalue_out[2],
        router_out[0],
        router_out[1],
        router_out[2],
        gain_out[0],
        gain_out[1],
        gain_out[2],
        embed_out[0],
        embed_out[1],
        embed_out[2],
    )


def solution(mesh):
    in_specs = (
        P("group", None, "dp", "tensor"),
        P(None, "dp", "tensor"),
        P(None, "dp", "tensor"),
        P("group", "dp", None),
        P("dp", None),
        P("dp", None),
        P("group", None, "dp"),
        P(None, "dp"),
        P(None, "dp"),
        P("group", "dp", "tensor"),
        P("dp", "tensor"),
        P("dp", "tensor"),
        P("tensor", None),
        P(),
    )
    out_specs = (
        P(None, "dp", "tensor"),
        P(None, "dp", "tensor"),
        P(None, "dp", "tensor"),
        P("dp", None),
        P("dp", None),
        P("dp", None),
        P(None, "dp"),
        P(None, "dp"),
        P(None, "dp"),
        P("dp", "tensor"),
        P("dp", "tensor"),
        P("dp", "tensor"),
    )
    return jax.shard_map(local, mesh=mesh, in_specs=in_specs, out_specs=out_specs, check_vma=False)
```

profile of v0, /device:TPU:63, one launch (start us, length us, event | category | flops | bytes accessed | tf_op | source)
XLA Modules:
  0.0 511.7 jit_solution(6677557871619569564)
XLA Ops:
  7.2 0.0 copy-start
  7.2 0.0 reduce-scatter.12.cloned.1.call-start
  7.2 0.0 copy-start.6
  7.2 0.0 copy-start.7
  7.3 0.7 bitcast_subtract_fusion.4
  8.0 0.0 copy-start.2
  8.0 0.0 copy-start.3
  8.0 0.9 copy.46
  8.9 0.0 reduce-scatter.12.cloned.1.call-update
  8.9 0.0 reduce-scatter.10.cloned.1.call-start
  8.9 0.0 copy-done.6
  8.9 0.0 copy-done.7
  9.0 0.8 copy.44
  9.8 0.0 reduce-scatter.10.cloned.1.call-update
  9.8 0.0 reduce-scatter.8.cloned.1.call-start
  9.9 0.0 copy-done.2
  9.9 0.0 copy-done.3
  9.9 0.8 bitcast_subtract_fusion
  10.8 0.0 copy-start.1
  10.8 0.0 copy-start.4
  10.8 0.0 reduce-scatter.8.cloned.1.call-update
  11.5 0.0 copy-done
  11.5 0.2 copy-done.1
  11.7 0.1 copy-done.4
  11.8 0.0 copy-start.5
  11.8 0.4 fusion
  12.2 342.6 %psum.7 = f32[125,64]{0,1:T(8,128)S(1)} all-reduce(f32[125,64]{0,1:T(8,128)S(1)} %fusion), channel_id=1, replica_groups=mesh['group'=8,'dp'=8,'tensor'=8] {'group','tensor'}, use_global_device_ids=true, to_apply=%region_3.0 | all-reduce | flops 8000 | bytes 64000 | tf_op jit(solution)/shard_map/psum | solution.py:84
  354.8 0.0 copy-done.5
  354.8 1.3 multiply_subtract_fusion
  356.1 0.0 reduce-scatter.12.cloned.1.call-done
  356.1 0.8 copy.47
  356.9 0.8 fusion.9
  357.7 32.8 %all-gather.5 = f32[8,64,2]{1,2,0:T(2,128)S(1)} all-gather(f32[1,64,2]{1,2,0:T(2,128)S(1)} %get-tuple-element.19), channel_id=1, replica_groups=mesh['group'=8,'dp'=8,'tensor'=8] {'group'}, dimensions={0}, use_global_device_ids=true | all-gather | bytes 4608 | tf_op jit(solution)/shard_map/all_gather | solution.py:73
  390.5 0.7 reshape.35
  391.2 8.7 %all-gather.4 = f32[8,64,2]{1,2,0:T(2,128)S(1)} all-gather(f32[1,64,2]{1,2,0:T(2,128)S(1)} %get-tuple-element.20), channel_id=1, replica_groups=mesh['group'=8,'dp'=8,'tensor'=8] {'group'}, dimensions={0}, use_global_device_ids=true | all-gather | bytes 4608 | tf_op jit(solution)/shard_map/all_gather | solution.py:72
  399.9 0.7 reshape.33
  400.6 10.1 %all-gather.3 = f32[8,64,2]{1,2,0:T(2,128)S(1)} all-gather(f32[1,64,2]{1,2,0:T(2,128)S(1)} %get-tuple-element.22), channel_id=1, replica_groups=mesh['group'=8,'dp'=8,'tensor'=8] {'group'}, dimensions={0}, use_global_device_ids=true | all-gather | bytes 4608 | tf_op jit(solution)/shard_map/all_gather | solution.py:71
  410.6 0.7 reshape.31
  411.3 0.0 reduce-scatter.10.cloned.1.call-done
  411.3 0.8 copy.45
  412.1 0.8 subtract_bitcast_fusion
  412.9 14.1 %all-gather.2 = f32[8,64,8]{1,2,0:T(8,128)S(1)} all-gather(f32[1,64,8]{1,2,0:T(8,128)S(1)} %get-tuple-element.17), channel_id=1, replica_groups=mesh['group'=8,'dp'=8,'tensor'=8] {'group'}, dimensions={0}, use_global_device_ids=true | all-gather | bytes 18432 | tf_op jit(solution)/shard_map/all_gather | solution.py:70
  427.0 0.7 reshape.29
  427.7 14.1 %all-gather.1 = f32[8,64,8]{1,2,0:T(8,128)S(1)} all-gather(f32[1,64,8]{1,2,0:T(8,128)S(1)} %get-tuple-element.18), channel_id=1, replica_groups=mesh['group'=8,'dp'=8,'tensor'=8] {'group'}, dimensions={0}, use_global_device_ids=true | all-gather | bytes 18432 | tf_op jit(solution)/shard_map/all_gather | solution.py:69
  441.7 0.7 reshape.27
  442.4 14.1 %all-gather = f32[8,64,8]{1,2,0:T(8,128)S(1)} all-gather(f32[1,64,8]{1,2,0:T(8,128)S(1)} %get-tuple-element.21), channel_id=1, replica_groups=mesh['group'=8,'dp'=8,'tensor'=8] {'group'}, dimensions={0}, use_global_device_ids=true | all-gather | bytes 18432 | tf_op jit(solution)/shard_map/all_gather | solution.py:68
  456.5 0.7 reshape.25
  457.2 0.0 reduce-scatter.8.cloned.1.call-done
  457.2 0.9 multiply_subtract_fusion.1
  458.1 14.9 %all_gather.29 = f32[2,512,128]{2,1,0:T(8,128)S(1)} all-gather(f32[2,64,128]{2,1,0:T(8,128)S(1)} %get-tuple-element.14), channel_id=1, replica_groups=mesh['group'=8,'dp'=8,'tensor'=8] {'group'}, dimensions={1}, use_global_device_ids=true | all-gather | bytes 589824 | tf_op jit(solution)/shard_map/all_gather | solution.py:67
  473.0 14.9 %all_gather.28 = f32[2,512,128]{2,1,0:T(8,128)S(1)} all-gather(f32[2,64,128]{2,1,0:T(8,128)S(1)} %get-tuple-element.15), channel_id=1, replica_groups=mesh['group'=8,'dp'=8,'tensor'=8] {'group'}, dimensions={1}, use_global_device_ids=true | all-gather | bytes 589824 | tf_op jit(solution)/shard_map/all_gather | solution.py:66
  487.9 14.9 %all_gather.27 = f32[2,512,128]{2,1,0:T(8,128)S(1)} all-gather(f32[2,64,128]{2,1,0:T(8,128)S(1)} %get-tuple-element.16), channel_id=1, replica_groups=mesh['group'=8,'dp'=8,'tensor'=8] {'group'}, dimensions={1}, use_global_device_ids=true | all-gather | bytes 589824 | tf_op jit(solution)/shard_map/all_gather | solution.py:65
  502.8 0.8 copy.57
  503.6 0.8 copy.58
  504.4 0.8 copy.59
  (7 shorter events, 0.0 us)
Async XLA Ops:
  7.2 4.3 copy-start
  7.2 348.9 %reduce-scatter.12.cloned.1.call-start = ((), (), s32[]{:S(2)}) async-start(), calls=%async_computation.5 | async-start | bytes 294912
  7.2 1.7 copy-start.6
  7.2 1.7 copy-start.7
  8.0 1.9 copy-start.2
  8.0 1.9 copy-start.3
  8.9 402.4 %reduce-scatter.10.cloned.1.call-start = ((), (), s32[]{:S(2)}) async-start(), calls=%async_computation.4 | async-start | bytes 294912
  9.8 447.4 %reduce-scatter.8.cloned.1.call-start = ((), (), s32[]{:S(2)}) async-start(), calls=%async_computation.3 | async-start | bytes 589824 | tf_op jit(solution)/shard_map/reduce_scatter | solution.py:38
  10.8 0.9 copy-start.1
  10.8 1.0 copy-start.4
  11.8 343.0 %copy-start.5 = (f32[125,512]{1,0:T(8,128)S(1)}, f32[125,512]{1,0:T(8,128)}, u32[]{:S(2)}) copy-start(f32[125,512]{1,0:T(8,128)} %param.25) | copy-start | bytes 768004
Sparse Core Ops, SparseCore 0:
  11.4 40.1 reduce-scatter.11
  54.9 37.6 reduce-scatter.9
  96.0 38.3 reduce-scatter.7
where the time goes:
time: 512 us
  blocking collectives  481 us (94%)
  between operations  14.6 us (3%)
  local copies, waits for them, and re-layouts  10.1 us (2%)
    psum x1, blocking collectives, local(): factors = lax.psum(partial_factors, ('group', 'tensor'))  343 us
    all_gather x1, blocking collectives, local(): lax.all_gather(gain_part[2], 'group', axis=1, tiled=True)  32.8 us
    all_gather x1, blocking collectives, local(): lax.all_gather(keyvalue_part[2], 'group', axis=1, tiled=True)  14.9 us
    all_gather x1, blocking collectives, local(): lax.all_gather(keyvalue_part[1], 'group', axis=1, tiled=True)  14.9 us
    all_gather x1, blocking collectives, local(): lax.all_gather(keyvalue_part[0], 'group', axis=1, tiled=True)  14.9 us
    all_gather x1, blocking collectives, local(): lax.all_gather(router_part[2], 'group', axis=0, tiled=True)  14.1 us
    all_gather x1, blocking collectives, local(): lax.all_gather(router_part[0], 'group', axis=0, tiled=True)  14.1 us
    all_gather x1, blocking collectives, local(): lax.all_gather(router_part[1], 'group', axis=0, tiled=True)  14.1 us
  transfers between devices with their start and end apart: 3, of which 0 were waited for; matrix products, arithmetic and copies ran while one was open for 2% of the time, Pallas kernels for 0%

commit v1 on v0

--- a/solution.py
+++ b/solution.py
@@ -62,7 +62,15 @@
         outer_rate,
     )
     gathered = (
-        lax.all_gather(keyvalue_part[0], "group", axis=1, tiled=True),
+        jnp.concatenate(
+            jax.lax.all_to_all(
+                jnp.stack(jax.lax.axis_size("group") * [keyvalue_part[0]]),
+                axis_name="group",
+                concat_axis=0,
+                split_axis=0,
+            ),
+            axis=1,
+        ),
         lax.all_gather(keyvalue_part[1], "group", axis=1, tiled=True),
         lax.all_gather(keyvalue_part[2], "group", axis=1, tiled=True),
         lax.all_gather(router_part[0], "group", axis=0, tiled=True),

time: 512 us -> 509 us (level)
  the two profiles are of different devices: /device:TPU:63 before, /device:TPU:31 now
where the time goes in v1:
time: 509 us
  blocking collectives  450 us (88%)
  starting transfers between devices  25.8 us (5%)
  between operations  14.5 us (3%)
  local copies, waits for them, and re-layouts  11.4 us (2%)
  other arithmetic  5.12 us (1%)
    psum x1, blocking collectives, local(): factors = lax.psum(partial_factors, ('group', 'tensor'))  343 us
    all_to_all x1, starting transfers between devices, local(): jax.lax.all_to_all(jnp.stack(jax.lax.axis_size('group') * [keyvalue_part[...  25.7 us
    all_gather x1, blocking collectives, local(): lax.all_gather(gain_part[2], 'group', axis=1, tiled=True)  15.3 us
    all_gather x1, blocking collectives, local(): lax.all_gather(keyvalue_part[1], 'group', axis=1, tiled=True)  14.8 us
    all_gather x1, blocking collectives, local(): lax.all_gather(keyvalue_part[2], 'group', axis=1, tiled=True)  14.8 us
    all_gather x1, blocking collectives, local(): lax.all_gather(router_part[2], 'group', axis=0, tiled=True)  14.1 us
    all_gather x1, blocking collectives, local(): lax.all_gather(router_part[1], 'group', axis=0, tiled=True)  14.1 us
    all_gather x1, blocking collectives, local(): lax.all_gather(router_part[0], 'group', axis=0, tiled=True)  14.1 us
  transfers between devices with their start and end apart: 4, of which 0 were waited for; matrix products, arithmetic and copies ran while one was open for 3% of the time, Pallas kernels for 0%

profile of v1, /device:TPU:31, one launch (start us, length us, event | category | flops | bytes accessed | tf_op | source)
XLA Modules:
  0.0 508.8 jit_solution(12624684738381875045)
XLA Ops:
  7.2 0.0 copy-start
  7.2 0.0 copy-start.2
  7.2 0.0 reduce-scatter.12.cloned.1.call-start
  7.2 0.8 bitcast_subtract_fusion.4
  8.0 0.9 copy.47
  8.9 0.0 reduce-scatter.12.cloned.1.call-update
  8.9 0.0 reduce-scatter.8.cloned.1.call-start
  9.0 0.0 copy-done.2
  9.0 1.9 bitcast_subtract_fusion
  10.9 0.0 copy-start.5
  10.9 0.0 copy-start.6
  10.9 0.0 reduce-scatter.8.cloned.1.call-update
  10.9 0.0 reduce-scatter.10.cloned.1.call-start
  10.9 0.6 copy-done.5
  11.6 0.0 copy-done.6
  11.6 0.0 copy-start.1
  11.6 0.0 copy-start.3
  11.6 0.8 copy.45
  12.4 0.0 reduce-scatter.10.cloned.1.call-update
  13.1 0.0 copy-done
  13.1 0.0 copy-done.1
  13.1 0.0 copy-done.3
  13.2 0.0 copy-start.4
  13.2 0.4 fusion
  13.6 342.6 %psum.7 = f32[125,64]{0,1:T(8,128)S(1)} all-reduce(f32[125,64]{0,1:T(8,128)S(1)} %fusion), channel_id=1, replica_groups=mesh['group'=8,'dp'=8,'tensor'=8] {'group','tensor'}, use_global_device_ids=true, to_apply=%region_3.0 | all-reduce | flops 8000 | bytes 64000 | tf_op jit(solution)/shard_map/psum | solution.py:92
  356.2 0.0 copy-done.4
  356.2 1.3 multiply_subtract_fusion
  357.5 0.0 reduce-scatter.12.cloned.1.call-done
  357.5 0.8 copy.48
  358.3 0.0 reduce-scatter.8.cloned.1.call-done
  358.3 0.9 multiply_subtract_fusion.1
  359.2 0.8 stack.2
  360.1 25.7 %all-to-all-start = ((f32[8,2,64,128]{3,2,1,0:T(8,128)}), f32[8,2,64,128]{3,2,1,0:T(8,128)S(1)}, u32[]{:S(2)}, u32[]{:S(2)}) async-start(f32[8,2,64,128]{3,2,1,0:T(8,128)} %stack.2), calls=%async_computation.1 | async-start | bytes 1048576 | tf_op jit(solution)/shard_map/all_to_all | solution.py:66
  385.8 0.8 fusion.9
  386.5 15.3 %all-gather.5 = f32[8,64,2]{1,2,0:T(2,128)S(1)} all-gather(f32[1,64,2]{1,2,0:T(2,128)S(1)} %get-tuple-element.19), channel_id=1, replica_groups=mesh['group'=8,'dp'=8,'tensor'=8] {'group'}, dimensions={0}, use_global_device_ids=true | all-gather | bytes 4608 | tf_op jit(solution)/shard_map/all_gather | solution.py:81
  401.8 0.7 reshape.45
  402.5 11.8 %all-gather.4 = f32[8,64,2]{1,2,0:T(2,128)S(1)} all-gather(f32[1,64,2]{1,2,0:T(2,128)S(1)} %get-tuple-element.20), channel_id=1, replica_groups=mesh['group'=8,'dp'=8,'tensor'=8] {'group'}, dimensions={0}, use_global_device_ids=true | all-gather | bytes 4608 | tf_op jit(solution)/shard_map/all_gather | solution.py:80
  414.3 0.7 reshape.43
  414.9 8.7 %all-gather.3 = f32[8,64,2]{1,2,0:T(2,128)S(1)} all-gather(f32[1,64,2]{1,2,0:T(2,128)S(1)} %get-tuple-element.22), channel_id=1, replica_groups=mesh['group'=8,'dp'=8,'tensor'=8] {'group'}, dimensions={0}, use_global_device_ids=true | all-gather | bytes 4608 | tf_op jit(solution)/shard_map/all_gather | solution.py:79
  423.7 0.7 reshape.41
  424.3 0.0 reduce-scatter.10.cloned.1.call-done
  424.3 0.8 copy.46
  425.1 0.8 subtract_bitcast_fusion
  425.9 14.1 %all-gather.2 = f32[8,64,8]{1,2,0:T(8,128)S(1)} all-gather(f32[1,64,8]{1,2,0:T(8,128)S(1)} %get-tuple-element.17), channel_id=1, replica_groups=mesh['group'=8,'dp'=8,'tensor'=8] {'group'}, dimensions={0}, use_global_device_ids=true | all-gather | bytes 18432 | tf_op jit(solution)/shard_map/all_gather | solution.py:78
  440.0 0.7 reshape.39
  440.7 14.1 %all-gather.1 = f32[8,64,8]{1,2,0:T(8,128)S(1)} all-gather(f32[1,64,8]{1,2,0:T(8,128)S(1)} %get-tuple-element.18), channel_id=1, replica_groups=mesh['group'=8,'dp'=8,'tensor'=8] {'group'}, dimensions={0}, use_global_device_ids=true | all-gather | bytes 18432 | tf_op jit(solution)/shard_map/all_gather | solution.py:77
  454.8 0.7 reshape.37
  455.4 14.1 %all-gather = f32[8,64,8]{1,2,0:T(8,128)S(1)} all-gather(f32[1,64,8]{1,2,0:T(8,128)S(1)} %get-tuple-element.21), channel_id=1, replica_groups=mesh['group'=8,'dp'=8,'tensor'=8] {'group'}, dimensions={0}, use_global_device_ids=true | all-gather | bytes 18432 | tf_op jit(solution)/shard_map/all_gather | solution.py:76
  469.5 0.7 reshape.35
  470.2 14.8 %all_gather.25 = f32[2,512,128]{2,1,0:T(8,128)S(1)} all-gather(f32[2,64,128]{2,1,0:T(8,128)S(1)} %get-tuple-element.14), channel_id=1, replica_groups=mesh['group'=8,'dp'=8,'tensor'=8] {'group'}, dimensions={1}, use_global_device_ids=true | all-gather | bytes 589824 | tf_op jit(solution)/shard_map/all_gather | solution.py:75
  485.0 14.8 %all_gather.24 = f32[2,512,128]{2,1,0:T(8,128)S(1)} all-gather(f32[2,64,128]{2,1,0:T(8,128)S(1)} %get-tuple-element.15), channel_id=1, replica_groups=mesh['group'=8,'dp'=8,'tensor'=8] {'group'}, dimensions={1}, use_global_device_ids=true | all-gather | bytes 589824 | tf_op jit(solution)/shard_map/all_gather | solution.py:74
  499.8 0.0 all-to-all-done
  499.8 0.8 copy.38
  500.7 0.8 copy.57
  501.5 0.8 copy.58
  (7 shorter events, 0.0 us)
Async XLA Ops:
  7.2 5.9 %copy-start = (f32[512,64]{0,1:T(8,128)S(1)}, f32[512,64]{0,1:T(8,128)}, u32[]{:S(2)}) copy-start(f32[512,64]{0,1:T(8,128)} %param.26) | copy-start | bytes 393220
  7.2 1.8 copy-start.2
  7.2 350.3 %reduce-scatter.12.cloned.1.call-start = ((), (), s32[]{:S(2)}) async-start(), calls=%async_computation.6 | async-start | bytes 294912
  8.9 349.4 %reduce-scatter.8.cloned.1.call-start = ((), (), s32[]{:S(2)}) async-start(), calls=%async_computation.4 | async-start | bytes 589824 | tf_op jit(solution)/shard_map/reduce_scatter | solution.py:38
  10.9 0.7 copy-start.5
  10.9 0.7 copy-start.6
  10.9 413.4 %reduce-scatter.10.cloned.1.call-start = ((), (), s32[]{:S(2)}) async-start(), calls=%async_computation.5 | async-start | bytes 294912
  11.6 1.5 copy-start.1
  11.6 1.5 copy-start.3
  13.2 343.0 %copy-start.4 = (f32[125,512]{1,0:T(8,128)S(1)}, f32[125,512]{1,0:T(8,128)}, u32[]{:S(2)}) copy-start(f32[125,512]{1,0:T(8,128)} %param.25) | copy-start | bytes 768004
  360.1 139.7 %all-to-all-start = ((f32[8,2,64,128]{3,2,1,0:T(8,128)}), f32[8,2,64,128]{3,2,1,0:T(8,128)S(1)}, u32[]{:S(2)}, u32[]{:S(2)}) async-start(f32[8,2,64,128]{3,2,1,0:T(8,128)} %stack.2), calls=%async_computation.1 | async-start | bytes 1048576 | tf_op jit(solution)/shard_map/all_to_all | solution.py:66
Sparse Core Ops, SparseCore 0:
  11.4 40.4 reduce-scatter.11
  55.2 38.1 reduce-scatter.7
  96.8 37.6 reduce-scatter.9
